TPU v7x, 32 devices: a whole 2x2x4 slice. The times are simulated.
32 devices in a mesh: layer: 4 (over x, core), tok: 8 (over z, y).
Axes of the slice: x: 2, y: 2, z: 4, core: 2. Of those that a mesh axis runs over, the one named last changes fastest.
Arguments:
- active_codes: bfloat16 [4, 1024, 32], P('layer', 'tok'), may hold values from 0.19921875 to 3
- latent_ids: int32 [4, 1024, 32], P('layer', 'tok'), may hold values from 0 to 32767, as said below
- decoder: bfloat16 [4, 32768, 4096], P('layer', 'tok'), may hold values from -1 to 1
- carry_gain: float32 [4, 4096], P('layer'), may hold values from 0.1 to 1
- earlier_sum: bfloat16 [1024, 4096], P('tok'), may hold values from -6 to 6
- targets: bfloat16 [4, 1024, 4096], P('layer', 'tok'), may hold values from -6 to 6
Outputs:
- reconstruction: bfloat16 [4, 1024, 4096], P('layer', 'tok')
- code_grad: float32 [4, 1024, 32], P('layer', 'tok')
Inputs may be any that keep to these rules, and one draw needn't show every extreme that they name: `latent_ids`: A token's 32 ids in one layer are distinct. In each layer, the 128 tokens of one aligned block have at most 768 ids in any one range of 4096 consecutive latents, and in every layer one range holds exactly 768 ids of every block.
All inputs are finite; a program needn't handle non-finite values.
Results may differ from a plain program's by a relative error of at most 0.019.
Values may be sent and summed in bfloat16 or wider, within the bound.
No kernel may reach another device: no remote copies, remote signals or barrier semaphores. Data moves between devices by JAX's collectives and lax.ppermute only.
A program may use at most 256 MiB of HBM per device.

v0:
```python
import jax
import jax.numpy as jnp
from jax import lax
from jax.sharding import PartitionSpec as P


def prefix(shard, axis, combine, identity, reverse):
    length, mine = (lax.axis_size(axis), lax.axis_index(axis))
    everything = jax.tree.map(
        lambda part, kind: lax.all_gather(part.astype(kind), axis),
        shard,
        (jnp.bfloat16, jnp.bfloat16),
    )
    start = jax.tree.map(
        lambda part, zero: jnp.broadcast_to(jnp.asarray(zero, part.dtype), part.shape),
        shard,
        identity,
    )

    def lap(k, before):
        at = length - 1 - k if reverse else k
        reached = at > mine if reverse else at < mine
        new = combine(
            before, jax.tree.map(lambda part, own: part[at].astype(own.dtype), everything, shard)
        )
        return jax.tree.map(lambda a, b: jnp.where(reached, a, b), new, before)

    return lax.fori_loop(0, length, lap, start)


def bucket_lists(latent_rows, code_rows, range_size, owners, capacity):
    tok_rows, top_count = latent_rows.shape
    entries = tok_rows * top_count
    flat_ids = latent_rows.reshape(entries)
    owning = flat_ids // range_size
    within = flat_ids % range_size
    positions = jnp.arange(entries, dtype=jnp.int32) // top_count
    ordering = jnp.argsort(owning, stable=True)
    counts = jnp.sum(
        (owning[:, None] == jnp.arange(owners, dtype=jnp.int32)[None, :]).astype(jnp.int32), axis=0
    )
    starts = jnp.cumsum(counts) - counts
    sorted_rank = jnp.arange(entries, dtype=jnp.int32) - starts[owning[ordering]]
    rank_of = jnp.zeros(entries, jnp.int32).at[ordering].set(sorted_rank)
    slot_index = owning * capacity + rank_of
    slot_keys = (
        jnp.zeros(owners * capacity, jnp.int32).at[slot_index].set(within * tok_rows + positions)
    )
    slot_codes = (
        jnp.zeros(owners * capacity, jnp.bfloat16).at[slot_index].set(code_rows.reshape(entries))
    )
    return (slot_keys.reshape(owners, capacity), slot_codes.reshape(owners, capacity), slot_index)


def source_term(rows, slot_keys, slot_codes, tok_rows):
    token_index = slot_keys % tok_rows
    matches = token_index[None, :] == jnp.arange(tok_rows, dtype=jnp.int32)[:, None]
    spread = jnp.where(matches, slot_codes[None, :], jnp.zeros((), jnp.bfloat16))
    return jnp.dot(spread, rows, preferred_element_type=jnp.float32)


def slot_grads_of(rows, slot_keys, grad_block, tok_rows):
    token_index = slot_keys % tok_rows
    products = jnp.einsum("td,cd->tc", grad_block, rows, preferred_element_type=jnp.float32)
    matches = token_index[None, :] == jnp.arange(tok_rows, dtype=jnp.int32)[:, None]
    return jnp.sum(jnp.where(matches, products, 0.0), axis=0)


def compose(earlier_part, later_part):
    return (earlier_part[0] * later_part[0], later_part[0] * earlier_part[1] + later_part[1])


def on_device(active_codes, latent_ids, decoder, carry_gain, earlier_sum, targets):
    owners = lax.axis_size("tok")
    tok_rows = active_codes.shape[1]
    top_count = active_codes.shape[2]
    range_size = decoder.shape[1]
    model_width = decoder.shape[2]
    capacity = 3 * tok_rows * top_count // (2 * owners)
    weights = decoder[0]
    slot_keys, slot_codes, slot_index = bucket_lists(
        latent_ids[0], active_codes[0], range_size, owners, capacity
    )
    recv_keys, recv_codes = (
        lax.all_to_all(slot_keys, "tok", split_axis=0, concat_axis=0, tiled=True),
        lax.all_to_all(slot_codes, "tok", split_axis=0, concat_axis=0, tiled=True),
    )
    row_cache = jnp.take(weights, recv_keys // tok_rows, axis=0)

    def one_source(triple):
        return source_term(triple[2], triple[0], triple[1], tok_rows)

    keys_part = recv_keys
    rows_part = row_cache
    term_blocks = lax.map(one_source, (keys_part, recv_codes, rows_part))
    decoded = lax.psum_scatter(
        term_blocks.reshape(lax.axis_size("tok") * tok_rows, model_width).astype(jnp.bfloat16),
        "tok",
        scatter_dimension=0,
        tiled=True,
    ).astype(jnp.float32)
    identity = (jnp.ones_like(carry_gain), jnp.zeros_like(decoded))
    ahead_gain, ahead_sum = prefix((carry_gain, decoded), "layer", compose, identity, False)
    recon_full = carry_gain * (ahead_gain * earlier_sum.astype(jnp.float32) + ahead_sum) + decoded
    misfit = recon_full - targets[0].astype(jnp.float32)
    behind_gain, behind_sum = prefix(
        (carry_gain, carry_gain * misfit), "layer", compose, identity, True
    )
    grad_low = (misfit + behind_sum).astype(jnp.bfloat16)

    def grads_of_source(triple):
        return slot_grads_of(triple[2], triple[0], triple[1], tok_rows)

    segment = lax.all_gather(grad_low, "tok", axis=0, tiled=True)
    source_count = segment.shape[0] // tok_rows
    keys_part = recv_keys
    rows_part = row_cache
    grad_blocks = segment.reshape(source_count, tok_rows, model_width)
    values = lax.map(grads_of_source, (keys_part, grad_blocks, rows_part))
    returned = lax.all_to_all(values, "tok", split_axis=0, concat_axis=0, tiled=True)
    code_grad = jnp.take(returned.reshape(owners * capacity), slot_index).reshape(
        tok_rows, top_count
    )
    return (recon_full.astype(jnp.bfloat16)[None], code_grad[None])


def solution(mesh):
    return jax.shard_map(
        on_device,
        mesh=mesh,
        in_specs=(
            P("layer", "tok", None),
            P("layer", "tok", None),
            P("layer", "tok", None),
            P("layer", None),
            P("tok", None),
            P("layer", "tok", None),
        ),
        out_specs=(P("layer", "tok", None), P("layer", "tok", None)),
        check_vma=False,
    )
```

profile of v0, /device:TPU:0, one launch (start us, length us, event | category | flops | bytes accessed | tf_op | source)
XLA Modules:
  0.0 932.6 jit_solution(17020449953633308792)
XLA Ops:
  7.2 0.8 copy.18
  8.4 0.7 fusion.49
  9.1 5.8 sort.17
  14.9 23.0 %gather_fusion = s32[4096]{0:T(1024)S(1)} fusion(s32[4096]{0:T(1024)S(1)} %add_select_fusion.3, s32[4096]{0:T(1024)S(1)} %get-tuple-element.481), kind=kCustom, calls=%fused_computation | custom fusion | bytes 49152 | tf_op jit(solution)/shard_map/gather | solution.py:43
  38.0 4.4 compare_select_fusion.7
  42.4 0.7 select_subtract_fusion
  43.0 15.5 %scatter_custom_fusion = s32[4096]{0:T(1024)S(1)} fusion(s32[4096]{0:T(1024)S(1)} %get-tuple-element.482, s32[4096]{0:T(1024)S(1)} %select_subtract_fusion, s32[]{:T(128)} %constant.237.clone.1), kind=kCustom, calls=%fused_computation.106 | custom fusion | bytes 16388 | tf_op jit(solution)/shard_map/scatter | solution.py:44
  58.6 0.6 broadcast_clamp_fusion.1
  59.4 28.6 %scatter_custom_fusion.2 = bf16[6144]{0:T(1024)(128)(2,1)S(1)} fusion(s32[4096]{0:T(1024)S(1)} %get-tuple-element.475, bf16[4096]{0:T(1024)(128)(2,1)S(1)} %reshape.307, bf16[]{:T(256)} %constant.252.clone.1), kind=kCustom, calls=%fused_computation.108 | custom fusion | bytes 12290 | tf_op jit(solution)/shard_map/scatter | solution.py:50
  88.5 0.7 reduce.8
  89.2 0.6 reshape.367
  89.9 7.3 all-to-all-start.1
  97.1 16.1 %scatter_custom_fusion.1 = s32[6144]{0:T(1024)} fusion(s32[4096]{0:T(1024)S(1)} %get-tuple-element.475, s32[4096]{0:T(1024)S(1)} %get-tuple-element.480, s32[]{:T(128)} %constant.237.clone.1), kind=kCustom, calls=%fused_computation.101 | custom fusion | bytes 24580 | tf_op jit(solution)/shard_map/scatter | solution.py:47
  113.2 6.0 all-to-all-start
  119.5 0.6 copy.29
  120.1 5.8 all-to-all-done
  126.0 262.2 %gather_fusion.1 = bf16[6144,4096]{1,0:T(8,128)(2,1)} fusion(bf16[4096,4096]{1,0:T(8,128)(2,1)} %bitcast.100, s32[6144]{0:T(1024)S(1)} %broadcast_clamp_fusion), kind=kCustom, calls=%fused_computation.1 | custom fusion | bytes 100687872 | tf_op jit(solution)/shard_map/jit(_take)/gather | solution.py:88
  388.3 33.4 %broadcast_select_fusion.2 = bf16[8,768,4096]{2,1,0:T(8,128)(2,1)} fusion(bf16[8,768,4096]{2,1,0:T(8,128)(2,1)} %bitcast.101, pred[8,768]{1,0:T(8,128)(4,1)S(1)} %compare_and_fusion), kind=kLoop, calls=%fused_computation.46 | loop fusion | flops 25165824 | bytes 100669440 | tf_op jit(solution)/shard_map/jit(_take)/select_n | solution.py:88
  421.7 44.3 %while.56 = (s32[]{:T(128)}, bf16[8,128,4096]{2,1,0:T(8,128)(2,1)}, s32[8,768]{1,0:T(8,128)S(1)}, bf16[8,768]{1,0:T(8,128)(2,1)}, bf16[8,768,4096]{2,1,0:T(8,128)(2,1)}, /*index=5*/s32[]{:T(128)}) while((s32[]{:T(128)}, bf16[8,128,4096]{2,1,0:T(8,128)(2,1)}, s32[8,768]{1,0:T(8,128)S(1)}, bf16[8,768]{1,0:T(8,128)(2,1)}, ...), condition=%wide.region_7.8_spmd, body=%wide.region_6.7_spmd.sunk | while | flops 805511424 | bytes 8403533 | solution.py:95
  421.7 0.7 dynamic-slice_reduce_fusion.2
  422.5 4.8 fusion.63
  427.2 0.7 dynamic-slice_reduce_fusion.2
  428.0 4.7 fusion.63
  432.7 0.7 dynamic-slice_reduce_fusion.2
  433.5 4.8 fusion.63
  438.3 0.7 dynamic-slice_reduce_fusion.2
  439.0 4.8 fusion.63
  443.8 0.7 dynamic-slice_reduce_fusion.2
  444.5 4.8 fusion.63
  449.3 0.7 dynamic-slice_reduce_fusion.2
  450.1 4.8 fusion.63
  454.9 0.7 dynamic-slice_reduce_fusion.2
  455.6 4.8 fusion.63
  460.4 0.7 dynamic-slice_reduce_fusion.2
  461.2 4.8 fusion.63
  466.0 159.1 %reduce-scatter.2.cloned.1.call-done = bf16[128,4096]{1,0:T(8,128)(2,1)} async-done(((bf16[1024,4096]{1,0:T(8,128)(2,1)}), bf16[128,4096]{1,0:T(8,128)(2,1)}) %reduce-scatter.2.cloned.1.call-update) | async-done | bytes 1048592 | tf_op jit(solution)/shard_map/reduce_scatter | solution.py:96
  625.2 5.2 all-gather.3
  630.5 29.8 %all-gather.10.cloned.1.call-done = bf16[512,4096]{1,0:T(8,128)(2,1)} async-done(((bf16[128,4096]{1,0:T(8,128)(2,1)}), bf16[512,4096]{1,0:T(8,128)(2,1)}) %all-gather.10.cloned.1.call-update) | async-done | bytes 4194320 | tf_op jit(solution)/shard_map/all_gather | solution.py:10
  660.2 10.5 %while.58 = (s32[]{:T(128)}, f32[1,4096]{1,0:T(1,128)S(1)}, f32[128,4096]{1,0:T(8,128)S(1)}, s32[]{:T(128)}, bf16[4,1,4096]{2,1,0:T(2,128)(2,1)S(1)}, /*index=5*/bf16[4,128,4096]{2,1,0:T(8,128)(2,1)}, s32[]{:T(128)}, s32[]{:T(128)}) while((s32[]{:T(128)}, f32[1,4096]{1,0:T(1,128)S(1)}, f32[128,4096]{1,0:T(8,128)S(1)}, ...), condition=%wide.region_10.11_spmd.clone, body=%wide.region_9.10_spmd.clone.sunk | while | flops 2637828 | bytes 5316723 | solution.py:28
  660.3 2.6 fusion.68
  663.0 2.6 fusion.68
  665.6 2.6 fusion.68
  668.2 2.6 fusion.68
  670.8 3.9 multiply_convert_fusion
  674.8 34.6 %all-gather.12.cloned.1.call-done = bf16[512,4096]{1,0:T(8,128)(2,1)} async-done(((bf16[128,4096]{1,0:T(8,128)(2,1)}), bf16[512,4096]{1,0:T(8,128)(2,1)}) %all-gather.12.cloned.1.call-update) | async-done | bytes 4194320 | tf_op jit(solution)/shard_map/all_gather | solution.py:10
  709.3 10.4 %while.59 = (s32[]{:T(128)}, f32[128,4096]{1,0:T(8,128)S(1)}, s32[]{:T(128)}, bf16[4,1,4096]{2,1,0:T(2,128)(2,1)S(1)}, bf16[4,128,4096]{2,1,0:T(8,128)(2,1)}, /*index=5*/s32[]{:T(128)}, s32[]{:T(128)}, s32[]{:T(128)}, s32[]{:T(128)}) while((s32[]{:T(128)}, f32[128,4096]{1,0:T(8,128)S(1)}, s32[]{:T(128)}, ...), condition=%wide.region_12.13_spmd.clone, body=%wide.region_11.12_spmd.clone.sunk | while | flops 2625544 | bytes 5284007 | solution.py:28
  709.4 2.6 fusion.69
  712.0 2.6 fusion.69
  714.6 2.6 fusion.69
  717.2 2.6 fusion.69
  719.8 4.1 add_convert_fusion
  723.9 125.1 %all-gather.8.cloned.1.call-done = bf16[1024,4096]{1,0:T(8,128)(2,1)} async-done(((bf16[128,4096]{1,0:T(8,128)(2,1)}), bf16[1024,4096]{1,0:T(8,128)(2,1)}) %all-gather.8.cloned.1.call-update) | async-done | bytes 8388624 | tf_op jit(solution)/shard_map/all_gather | solution.py:114
  849.0 44.0 %while.57 = (s32[]{:T(128)}, f32[8,768]{1,0:T(8,128)S(1)}, s32[8,768]{1,0:T(8,128)S(1)}, bf16[8,128,4096]{2,1,0:T(8,128)(2,1)}, bf16[8,768,4096]{2,1,0:T(8,128)(2,1)}, /*index=5*/s32[]{:T(128)}, s32[]{:T(128)}) while((s32[]{:T(128)}, f32[8,768]{1,0:T(8,128)S(1)}, s32[8,768]{1,0:T(8,128)S(1)}, bf16[8,128,4096]{2,1,0:T(8,128)(2,1)}, ...), condition=%wide.region_15.16_spmd, body=%wide.region_13.15_spmd.sunk | while | flops 805608960 | bytes 7365717 | solution.py:119
  849.0 5.3 fusion.67
  854.5 5.3 fusion.67
  860.0 5.3 fusion.67
  865.5 5.3 fusion.67
  871.0 5.3 fusion.67
  876.5 5.3 fusion.67
  882.0 5.3 fusion.67
  887.6 5.3 fusion.67
  893.0 9.2 all_to_all.37
  902.3 23.0 %gather_fusion.2 = f32[4096]{0:T(1024)S(1)} fusion(f32[6144]{0:T(1024)S(1)} %bitcast.99, s32[4096]{0:T(1024)S(1)} %copy-done.4), kind=kCustom, calls=%fused_computation.2 | custom fusion | bytes 49152 | tf_op jit(solution)/shard_map/jit(_take)/gather | solution.py:121
  925.4 0.7 copy.21
  (87 shorter events, 3.4 us)
Async XLA Ops:
  14.9 44.3 %copy-start.5 = (bf16[1,128,32]{1,2,0:T(8,128)(2,1)S(1)}, bf16[1,128,32]{1,2,0:T(8,128)(2,1)}, u32[]{:S(2)}) copy-start(bf16[1,128,32]{1,2,0:T(8,128)(2,1)} %param.14) | copy-start | bytes 24580
  59.2 60.3 %copy-start.2 = (s32[4096]{0:T(1024)}, s32[4096]{0:T(1024)S(1)}, u32[]{:S(2)}) copy-start(s32[4096]{0:T(1024)S(1)} %get-tuple-element.475) | copy-start | bytes 49156
  89.9 23.4 %all-to-all-start.1 = ((bf16[8,2,384]{2,1,0:T(2,128)(2,1)}), bf16[8,2,384]{2,1,0:T(2,128)(2,1)S(1)}, u32[]{:S(2)}, u32[]{:S(2)}) async-start(bf16[8,2,384]{2,1,0:T(2,128)(2,1)} %reshape.367), calls=%async_computation.1 | async-start | bytes 24576 | tf_op jit(solution)/shard_map/all_to_all | solution.py:86
  113.2 12.6 %all-to-all-start = ((s32[8,1,768]{2,1,0:T(1,128)}), s32[8,1,768]{2,1,0:T(1,128)S(1)}, u32[]{:S(2)}, u32[]{:S(2)}) async-start(s32[8,1,768]{2,1,0:T(1,128)} %bitcast.18), calls=%async_computation | async-start | bytes 49152 | tf_op jit(solution)/shard_map/all_to_all | solution.py:85
  119.2 505.9 %reduce-scatter.2.cloned.1.call-start = ((), (), s32[]{:S(2)}) async-start(), calls=%async_computation.4 | async-start | bytes 9437184 | tf_op jit(solution)/shard_map/reduce_scatter | solution.py:96
  466.0 159.2 %copy-start.1 = (f32[1,4096]{1,0:T(1,128)S(1)}, f32[1,4096]{1,0:T(1,128)}, u32[]{:S(2)}) copy-start(f32[1,4096]{1,0:T(1,128)} %param.17) | copy-start | bytes 49156
  466.0 194.3 %all-gather.10.cloned.1.call-start = ((), (), s32[]{:S(2)}) async-start(), calls=%async_computation.6 | async-start | bytes 5242880 | tf_op jit(solution)/shard_map/all_gather | solution.py:10
  625.1 84.2 %all-gather.12.cloned.1.call-start = ((), (), s32[]{:S(2)}) async-start(), calls=%async_computation.7 | async-start | bytes 5242880 | tf_op jit(solution)/shard_map/all_gather | solution.py:10
  660.2 10.6 %copy-start = (bf16[1,128,4096]{2,1,0:T(8,128)(2,1)S(1)}, bf16[1,128,4096]{2,1,0:T(8,128)(2,1)}, u32[]{:S(2)}) copy-start(bf16[1,128,4096]{2,1,0:T(8,128)(2,1)} %param.19) | copy-start | bytes 3145732
  674.7 174.3 %all-gather.8.cloned.1.call-start = ((), (), s32[]{:S(2)}) async-start(), calls=%async_computation.5 | async-start | bytes 9437184 | tf_op jit(solution)/shard_map/all_gather | solution.py:114
  849.0 53.3 %copy-start.4 = (s32[4096]{0:T(1024)S(1)}, s32[4096]{0:T(1024)}, u32[]{:S(2)}) copy-start(s32[4096]{0:T(1024)} %get-tuple-element.474) | copy-start | bytes 49156
  902.3 23.0 %copy-start.3 = (s32[4096]{0:T(1024)S(1)}, s32[4096]{0:T(1024)}, u32[]{:S(2)}) copy-start(s32[4096]{0:T(1024)} %copy-done.2) | copy-start | bytes 49156
Sparse Core Ops, SparseCore 0:
  466.1 158.9 reduce-scatter.1
  626.7 33.4 all-gather.9
  674.8 34.4 all-gather.11
  724.0 124.9 all-gather.7
where the time goes:
time: 940 us; the launch traced here: 933 us
  local copies, waits for them, and re-layouts  379 us (40%)
  waiting for transfers between devices  354 us (38%)
  matrix products  80.9 us (9%)
  other arithmetic  75.3 us (8%)
  blocking collectives  14.5 us (2%)
  between operations  14 us (1%)
  starting transfers between devices  13.6 us (1%)
    gather x1, local copies, waits for them, and re-layouts, on_device(): row_cache = jnp.take(weights, recv_keys // tok_rows, axis=0)  262 us
    reduce_scatter x1, waiting for transfers between devices, on_device(): lax.psum_scatter(term_blocks.reshape(lax.axis_size('tok') * tok_rows, mod...  159 us
    all_gather x1, waiting for transfers between devices, on_device(): segment = lax.all_gather(grad_low, 'tok', axis=0, tiled=True)  125 us
    all_gather x2, waiting for transfers between devices, prefix(): lax.all_gather(part.astype(kind), axis)  64.4 us
    dot_general x8, matrix products, slot_grads_of(): jnp.einsum('td,cd->tc', grad_block, rows, preferred_element_type=jnp.floa...  42.8 us
    dot_general x8, matrix products, source_term(): return jnp.dot(spread, rows, preferred_element_type=jnp.float32)  38.1 us
    select_n x2, other arithmetic, on_device(): row_cache = jnp.take(weights, recv_keys // tok_rows, axis=0)  33.5 us
    scatter x1, local copies, waits for them, and re-layouts, bucket_lists(): jnp.zeros(owners * capacity, jnp.bfloat16).at[slot_index]  28.6 us
  transfers between devices with their start and end apart: 6, of which 5 were waited for; matrix products, arithmetic and copies ran while one was open for 2% of the time, Pallas kernels for 0%

commit v1 on v0

--- a/solution.py
+++ b/solution.py
@@ -111,7 +111,15 @@
     def grads_of_source(triple):
         return slot_grads_of(triple[2], triple[0], triple[1], tok_rows)
 
-    segment = lax.all_gather(grad_low, "tok", axis=0, tiled=True)
+    ways, here = (lax.axis_size("tok"), lax.axis_index("tok"))
+    grown, reach = (grad_low, 1)
+    while reach < ways:
+        theirs = lax.ppermute(grown, "tok", [(d, d ^ reach) for d in range(ways)])
+        mine_first = jnp.concatenate([grown, theirs], axis=0)
+        theirs_first = jnp.concatenate([theirs, grown], axis=0)
+        grown = jnp.where(here & reach == 0, mine_first, theirs_first)
+        reach = 2 * reach
+    segment = grown
     source_count = segment.shape[0] // tok_rows
     keys_part = recv_keys
     rows_part = row_cache

time: 940 us -> 1090 us (1.16)
  waiting for transfers between devices: 354 us -> 478 us
  other arithmetic: 75.3 us -> 93 us
    ppermute x0 -> x3, waiting for transfers between devices: none -> 249 us  [on_device(): theirs = lax.ppermute(grown, 'tok', [(d, d ^ reach) for d in range(ways)])]
    all_gather x1 -> x0, waiting for transfers between devices: 125 us -> none  [on_device(): segment = lax.all_gather(grad_low, 'tok', axis=0, tiled=True)]
    select_n x0 -> x3, other arithmetic: none -> 17.8 us  [on_device(): grown = jnp.where(here & reach == 0, mine_first, theirs_first)]
  transfers between devices with their start and end apart: 6 -> 8, of which waited for: 5 -> 7; matrix products, arithmetic and copies ran while one was open for 2% -> 2% of each run, Pallas kernels for 0% -> 0%
where the time goes in v1:
time: 1090 us; the launch traced here: 1080 us
  waiting for transfers between devices  478 us (44%)
  local copies, waits for them, and re-layouts  379 us (35%)
  other arithmetic  93 us (9%)
  matrix products  80.9 us (7%)
  starting transfers between devices  19 us (2%)
  blocking collectives  17.2 us (2%)
  between operations  14 us (1%)
    gather x1, local copies, waits for them, and re-layouts, on_device(): row_cache = jnp.take(weights, recv_keys // tok_rows, axis=0)  262 us
    ppermute x3, waiting for transfers between devices, on_device(): theirs = lax.ppermute(grown, 'tok', [(d, d ^ reach) for d in range(ways)])  249 us
    reduce_scatter x1, waiting for transfers between devices, on_device(): lax.psum_scatter(term_blocks.reshape(lax.axis_size('tok') * tok_rows, mod...  159 us
    all_gather x2, waiting for transfers between devices, prefix(): lax.all_gather(part.astype(kind), axis)  64.4 us
    dot_general x8, matrix products, slot_grads_of(): jnp.einsum('td,cd->tc', grad_block, rows, preferred_element_type=jnp.floa...  42.8 us
    dot_general x8, matrix products, source_term(): return jnp.dot(spread, rows, preferred_element_type=jnp.float32)  38.1 us
    select_n x2, other arithmetic, on_device(): row_cache = jnp.take(weights, recv_keys // tok_rows, axis=0)  33.5 us
    scatter x1, local copies, waits for them, and re-layouts, bucket_lists(): jnp.zeros(owners * capacity, jnp.bfloat16).at[slot_index]  28.6 us
  transfers between devices with their start and end apart: 8, of which 7 were waited for; matrix products, arithmetic and copies ran while one was open for 2% of the time, Pallas kernels for 0%

profile of v1, /device:TPU:0, one launch (start us, length us, event | category | flops | bytes accessed | tf_op | source)
XLA Modules:
  0.0 1082.6 jit_solution(16874490248339815755)
XLA Ops:
  7.2 0.8 copy.18
  9.1 5.8 sort.17
  14.9 23.0 %gather_fusion = s32[4096]{0:T(1024)S(1)} fusion(s32[4096]{0:T(1024)S(1)} %add_select_fusion.3, s32[4096]{0:T(1024)S(1)} %get-tuple-element.481), kind=kCustom, calls=%fused_computation | custom fusion | bytes 49152 | tf_op jit(solution)/shard_map/gather | solution.py:43
  38.0 4.4 compare_select_fusion.7
  43.0 15.5 %scatter_custom_fusion = s32[4096]{0:T(1024)S(1)} fusion(s32[4096]{0:T(1024)S(1)} %get-tuple-element.482, s32[4096]{0:T(1024)S(1)} %select_subtract_fusion, s32[]{:T(128)} %constant.242.clone.1), kind=kCustom, calls=%fused_computation.109 | custom fusion | bytes 16388 | tf_op jit(solution)/shard_map/scatter | solution.py:44
  59.4 28.6 %scatter_custom_fusion.2 = bf16[6144]{0:T(1024)(128)(2,1)S(1)} fusion(s32[4096]{0:T(1024)S(1)} %get-tuple-element.475, bf16[4096]{0:T(1024)(128)(2,1)S(1)} %reshape.308, bf16[]{:T(256)} %constant.257.clone.1), kind=kCustom, calls=%fused_computation.111 | custom fusion | bytes 12290 | tf_op jit(solution)/shard_map/scatter | solution.py:50
  89.9 7.3 all-to-all-start.1
  97.1 16.1 %scatter_custom_fusion.1 = s32[6144]{0:T(1024)} fusion(s32[4096]{0:T(1024)S(1)} %get-tuple-element.475, s32[4096]{0:T(1024)S(1)} %get-tuple-element.480, s32[]{:T(128)} %constant.242.clone.1), kind=kCustom, calls=%fused_computation.104 | custom fusion | bytes 24580 | tf_op jit(solution)/shard_map/scatter | solution.py:47
  113.2 6.0 all-to-all-start
  120.1 5.8 all-to-all-done
  126.0 262.2 %gather_fusion.1 = bf16[6144,4096]{1,0:T(8,128)(2,1)} fusion(bf16[4096,4096]{1,0:T(8,128)(2,1)} %bitcast.100, s32[6144]{0:T(1024)S(1)} %broadcast_clamp_fusion), kind=kCustom, calls=%fused_computation.1 | custom fusion | bytes 100687872 | tf_op jit(solution)/shard_map/jit(_take)/gather | solution.py:88
  388.3 33.4 %broadcast_select_fusion.2 = bf16[8,768,4096]{2,1,0:T(8,128)(2,1)} fusion(bf16[8,768,4096]{2,1,0:T(8,128)(2,1)} %bitcast.101, pred[8,768]{1,0:T(8,128)(4,1)S(1)} %compare_and_fusion), kind=kLoop, calls=%fused_computation.46 | loop fusion | flops 25165824 | bytes 100669440 | tf_op jit(solution)/shard_map/jit(_take)/select_n | solution.py:88
  421.7 44.3 %while.56 = (s32[]{:T(128)}, bf16[8,128,4096]{2,1,0:T(8,128)(2,1)}, s32[8,768]{1,0:T(8,128)S(1)}, bf16[8,768]{1,0:T(8,128)(2,1)}, bf16[8,768,4096]{2,1,0:T(8,128)(2,1)}, /*index=5*/s32[]{:T(128)}) while((s32[]{:T(128)}, bf16[8,128,4096]{2,1,0:T(8,128)(2,1)}, s32[8,768]{1,0:T(8,128)S(1)}, bf16[8,768]{1,0:T(8,128)(2,1)}, ...), condition=%wide.region_7.8_spmd, body=%wide.region_6.7_spmd.sunk | while | flops 805511424 | bytes 8403533 | solution.py:95
  421.7 0.7 dynamic-slice_reduce_fusion.2
  422.5 4.8 fusion.63
  427.2 0.7 dynamic-slice_reduce_fusion.2
  428.0 4.7 fusion.63
  432.7 0.7 dynamic-slice_reduce_fusion.2
  433.5 4.8 fusion.63
  438.3 0.7 dynamic-slice_reduce_fusion.2
  439.0 4.8 fusion.63
  443.8 0.7 dynamic-slice_reduce_fusion.2
  444.5 4.8 fusion.63
  449.3 0.7 dynamic-slice_reduce_fusion.2
  450.1 4.8 fusion.63
  455.6 4.8 fusion.63
  460.4 0.7 dynamic-slice_reduce_fusion.2
  461.2 4.8 fusion.63
  466.0 159.1 %reduce-scatter.2.cloned.1.call-done = bf16[128,4096]{1,0:T(8,128)(2,1)} async-done(((bf16[1024,4096]{1,0:T(8,128)(2,1)}), bf16[128,4096]{1,0:T(8,128)(2,1)}) %reduce-scatter.2.cloned.1.call-update) | async-done | bytes 1048592 | tf_op jit(solution)/shard_map/reduce_scatter | solution.py:96
  625.2 5.2 all-gather.3
  630.5 29.8 %all-gather.7.cloned.1.call-done = bf16[512,4096]{1,0:T(8,128)(2,1)} async-done(((bf16[128,4096]{1,0:T(8,128)(2,1)}), bf16[512,4096]{1,0:T(8,128)(2,1)}) %all-gather.7.cloned.1.call-update) | async-done | bytes 4194320 | tf_op jit(solution)/shard_map/all_gather | solution.py:10
  660.2 10.5 while.58
  660.3 2.6 fusion.68
  663.0 2.6 fusion.68
  665.6 2.6 fusion.68
  668.2 2.6 fusion.68
  670.8 3.9 multiply_convert_fusion
  674.7 34.6 %all-gather.9.cloned.1.call-done = bf16[512,4096]{1,0:T(8,128)(2,1)} async-done(((bf16[128,4096]{1,0:T(8,128)(2,1)}), bf16[512,4096]{1,0:T(8,128)(2,1)}) %all-gather.9.cloned.1.call-update) | async-done | bytes 4194320 | tf_op jit(solution)/shard_map/all_gather | solution.py:10
  709.3 10.4 while.59
  709.4 2.6 fusion.69
  712.0 2.6 fusion.69
  714.6 2.6 fusion.69
  717.2 2.6 fusion.69
  719.8 4.0 add_convert_fusion
  723.7 1.5 collective-permute-start
  725.2 23.9 %collective-permute-done = bf16[128,4096]{1,0:T(8,128)(2,1)} collective-permute-done((bf16[128,4096]{1,0:T(8,128)(2,1)S(1)}, bf16[128,4096]{1,0:T(8,128)(2,1)}, u32[]{:S(2)}, u32[]{:S(2)}) %collective-permute-start) | collective-permute-done | bytes 1048608 | tf_op jit(solution)/shard_map/ppermute | solution.py:117
  749.2 2.3 maximum_select_fusion.2
  751.4 1.6 collective-permute-start.1
  753.0 45.6 %collective-permute-done.1 = bf16[256,4096]{1,0:T(8,128)(2,1)} collective-permute-done((bf16[256,4096]{1,0:T(8,128)(2,1)S(1)}, bf16[256,4096]{1,0:T(8,128)(2,1)}, u32[]{:S(2)}, u32[]{:S(2)}) %collective-permute-start.1) | collective-permute-done | bytes 2097184 | tf_op jit(solution)/shard_map/ppermute | solution.py:117
  798.6 4.7 maximum_select_fusion.1
  803.2 2.4 collective-permute-start.2
  805.6 179.7 %collective-permute-done.2 = bf16[512,4096]{1,0:T(8,128)(2,1)} collective-permute-done((bf16[512,4096]{1,0:T(8,128)(2,1)}, bf16[512,4096]{1,0:T(8,128)(2,1)}, u32[]{:S(2)}, u32[]{:S(2)}) %collective-permute-start.2) | collective-permute-done | bytes 4194336 | tf_op jit(solution)/shard_map/ppermute | solution.py:117
  985.3 10.9 %maximum_select_fusion = bf16[1024,4096]{1,0:T(8,128)(2,1)} fusion(bf16[512,4096]{1,0:T(8,128)(2,1)} %collective-permute-done.2, bf16[512,4096]{1,0:T(8,128)(2,1)} %maximum_select_fusion.1, pred[]{:T(512)S(6)} %eq.82), kind=kLoop, calls=%fused_computation.47 | loop fusion | flops 37748736 | bytes 16777216 | tf_op jit(solution)/shard_map/jit(_where)/select_n | solution.py:120
  996.2 44.0 %while.57 = (s32[]{:T(128)}, f32[8,768]{1,0:T(8,128)S(1)}, s32[8,768]{1,0:T(8,128)S(1)}, bf16[8,128,4096]{2,1,0:T(8,128)(2,1)}, bf16[8,768,4096]{2,1,0:T(8,128)(2,1)}, /*index=5*/s32[]{:T(128)}, s32[]{:T(128)}) while((s32[]{:T(128)}, f32[8,768]{1,0:T(8,128)S(1)}, s32[8,768]{1,0:T(8,128)S(1)}, bf16[8,128,4096]{2,1,0:T(8,128)(2,1)}, ...), condition=%wide.region_15.16_spmd, body=%wide.region_13.15_spmd.sunk | while | flops 805608960 | bytes 7365717 | solution.py:127
  996.2 5.3 fusion.67
  1001.8 5.3 fusion.67
  1007.3 5.3 fusion.67
  1012.8 5.3 fusion.67
  1018.3 5.3 fusion.67
  1023.8 5.3 fusion.67
  1029.3 5.3 fusion.67
  1034.8 5.3 fusion.67
  1040.3 11.9 %all_to_all.37 = f32[8,1,768]{2,1,0:T(1,128)S(1)} all-to-all(f32[8,1,768]{2,1,0:T(1,128)S(1)} %all_to_all.31), channel_id=1, replica_groups=mesh['layer'=4,'tok'=8] {'tok'}, dimensions={0} | all-to-all | bytes 49152 | tf_op jit(solution)/shard_map/all_to_all | solution.py:128
  1052.2 23.0 %gather_fusion.2 = f32[4096]{0:T(1024)S(1)} fusion(f32[6144]{0:T(1024)S(1)} %bitcast.99, s32[4096]{0:T(1024)S(1)} %copy-done.4), kind=kCustom, calls=%fused_computation.2 | custom fusion | bytes 49152 | tf_op jit(solution)/shard_map/jit(_take)/gather | solution.py:129
  (93 shorter events, 8.6 us)
Async XLA Ops:
  14.9 44.3 %copy-start.5 = (bf16[1,128,32]{1,2,0:T(8,128)(2,1)S(1)}, bf16[1,128,32]{1,2,0:T(8,128)(2,1)}, u32[]{:S(2)}) copy-start(bf16[1,128,32]{1,2,0:T(8,128)(2,1)} %param.14) | copy-start | bytes 24580
  59.2 60.3 %copy-start.2 = (s32[4096]{0:T(1024)}, s32[4096]{0:T(1024)S(1)}, u32[]{:S(2)}) copy-start(s32[4096]{0:T(1024)S(1)} %get-tuple-element.475) | copy-start | bytes 49156
  89.9 23.4 %all-to-all-start.1 = ((bf16[8,2,384]{2,1,0:T(2,128)(2,1)}), bf16[8,2,384]{2,1,0:T(2,128)(2,1)S(1)}, u32[]{:S(2)}, u32[]{:S(2)}) async-start(bf16[8,2,384]{2,1,0:T(2,128)(2,1)} %reshape.368), calls=%async_computation.1 | async-start | bytes 24576 | tf_op jit(solution)/shard_map/all_to_all | solution.py:86
  113.2 12.6 %all-to-all-start = ((s32[8,1,768]{2,1,0:T(1,128)}), s32[8,1,768]{2,1,0:T(1,128)S(1)}, u32[]{:S(2)}, u32[]{:S(2)}) async-start(s32[8,1,768]{2,1,0:T(1,128)} %bitcast.18), calls=%async_computation | async-start | bytes 49152 | tf_op jit(solution)/shard_map/all_to_all | solution.py:85
  119.2 505.9 %reduce-scatter.2.cloned.1.call-start = ((), (), s32[]{:S(2)}) async-start(), calls=%async_computation.4 | async-start | bytes 9437184 | tf_op jit(solution)/shard_map/reduce_scatter | solution.py:96
  466.0 159.2 %copy-start.1 = (f32[1,4096]{1,0:T(1,128)S(1)}, f32[1,4096]{1,0:T(1,128)}, u32[]{:S(2)}) copy-start(f32[1,4096]{1,0:T(1,128)} %param.17) | copy-start | bytes 49156
  466.0 194.3 %all-gather.7.cloned.1.call-start = ((), (), s32[]{:S(2)}) async-start(), calls=%async_computation.5 | async-start | bytes 5242880 | tf_op jit(solution)/shard_map/all_gather | solution.py:10
  625.1 84.2 %all-gather.9.cloned.1.call-start = ((), (), s32[]{:S(2)}) async-start(), calls=%async_computation.6 | async-start | bytes 5242880 | tf_op jit(solution)/shard_map/all_gather | solution.py:10
  660.2 10.6 copy-start
  723.7 25.4 %collective-permute-start = (bf16[128,4096]{1,0:T(8,128)(2,1)S(1)}, bf16[128,4096]{1,0:T(8,128)(2,1)}, u32[]{:S(2)}, u32[]{:S(2)}) collective-permute-start(bf16[128,4096]{1,0:T(8,128)(2,1)S(1)} %get-tuple-element.478), channel_id=1, source_target_pairs={{0,1},{1,0},{2,3},{3,2},{4,5},{5,4},{6,7},{7,6},{8,9},{9,8},{10,11... | collective-permute-start | bytes 3145736 | tf_op jit(solution)/shard_map/ppermute | solution.py:117
  751.4 47.1 %collective-permute-start.1 = (bf16[256,4096]{1,0:T(8,128)(2,1)S(1)}, bf16[256,4096]{1,0:T(8,128)(2,1)}, u32[]{:S(2)}, u32[]{:S(2)}) collective-permute-start(bf16[256,4096]{1,0:T(8,128)(2,1)S(1)} %maximum_select_fusion.2), channel_id=1, source_target_pairs={{0,2},{1,3},{2,0},{3,1},{4,6},{5,7},{6,4},{7,5},{8,10},{9,11},{10,... | collective-permute-start | bytes 6291464 | tf_op jit(solution)/shard_map/ppermute | solution.py:117
  803.2 182.1 %collective-permute-start.2 = (bf16[512,4096]{1,0:T(8,128)(2,1)}, bf16[512,4096]{1,0:T(8,128)(2,1)}, u32[]{:S(2)}, u32[]{:S(2)}) collective-permute-start(bf16[512,4096]{1,0:T(8,128)(2,1)} %maximum_select_fusion.1), channel_id=1, source_target_pairs={{0,4},{1,5},{2,6},{3,7},{4,0},{5,1},{6,2},{7,3},{8,12},{9,13},{10,... | collective-permute-start | bytes 12582920 | tf_op jit(solution)/shard_map/ppermute | solution.py:117
  996.2 56.0 %copy-start.4 = (s32[4096]{0:T(1024)S(1)}, s32[4096]{0:T(1024)}, u32[]{:S(2)}) copy-start(s32[4096]{0:T(1024)} %get-tuple-element.474) | copy-start | bytes 49156
  1052.2 23.0 %copy-start.3 = (s32[4096]{0:T(1024)S(1)}, s32[4096]{0:T(1024)}, u32[]{:S(2)}) copy-start(s32[4096]{0:T(1024)} %copy-done.2) | copy-start | bytes 49156
Sparse Core Ops, SparseCore 0:
  466.1 158.9 reduce-scatter.1
  626.7 33.4 all-gather.6
  674.8 34.4 all-gather.8
